TPU v7x, 512 devices: a whole 4x4x16 slice. The times are simulated.
512 devices in a mesh: ctx: 64 (over z, y_lo, core), head: 8 (over x, y_hi).
Axes of the slice: x: 4, y: 4 (y_hi: 2, y_lo: 2; y = y_hi * 2 + y_lo), z: 16, core: 2. Of those that a mesh axis runs over, the one named last changes fastest.
Arguments:
- queries_nope: bfloat16 [4096, 8192], P('ctx', 'head'), may hold values from -4 to 4
- queries_rope: bfloat16 [4096, 4096], P('ctx', 'head'), may hold values from -128 to 128
- latents: bfloat16 [4096, 512], P('ctx'), may hold values from -8 to 8
- rope_keys: bfloat16 [4096, 64], P('ctx'), may hold values from -4 to 4
- positions: int32 [4096], P('ctx'), may hold values from 0 to 6143
- key_up: bfloat16 [512, 8192], P(None, 'head'), may hold values from -0.5 to 0.5
- value_up: bfloat16 [512, 8192], P(None, 'head'), may hold values from -0.25 to 0.25
- out_proj: bfloat16 [8192, 3584], P('head', 'ctx'), may hold values from -0.0625 to 0.0625
Outputs:
- attended: bfloat16 [4096, 3584], P('ctx', 'head')
All inputs are finite; a program needn't handle non-finite values.
Results may differ from a plain program's by a relative error of at most 0.014.
The roundings to bfloat16 on the way count: a program that leaves them out, or rounds other values in their place, can miss the bound.
Values may be sent and summed in bfloat16 or wider, within the bound.
No kernel may reach another device: no remote copies, remote signals or barrier semaphores. Data moves between devices by JAX's collectives and lax.ppermute only.
A program may use at most 64 MiB of HBM per device.

v0:
```python
import math
import jax
import jax.numpy as jnp
from jax import lax
from jax.sharding import PartitionSpec as P

LATENT = 512
ROPE = 64
NOPE = 128
VDIM = 128
masked_value = -1e30


def rope_tables(token_pos, width):
    half_width = width // 2
    freqs = jnp.exp(jnp.arange(half_width, dtype=jnp.float32) * (-2.0 * math.log(10000.0) / width))
    angle = token_pos.astype(jnp.float32)[:, None] * freqs[None, :]
    return (jnp.cos(angle), jnp.sin(angle))


def rotate(values, cosine, sine):
    half_width = values.shape[-1] // 2
    first_half = values[..., :half_width]
    second_half = values[..., half_width:]
    cos_part = cosine[:, None, :]
    sin_part = sine[:, None, :]
    return jnp.concatenate(
        [
            first_half * cos_part - second_half * sin_part,
            second_half * cos_part + first_half * sin_part,
        ],
        axis=-1,
    )


def attend(query_rows, query_index, keys, key_count):
    scale = 1.0 / math.sqrt(NOPE + ROPE)
    scores = jnp.einsum("rl,kl->rk", query_rows, keys, preferred_element_type=jnp.float32)
    key_index = lax.broadcasted_iota(jnp.int32, (1, key_count), 1)
    visible = key_index <= query_index[:, None]
    scores = jnp.where(visible, scores * scale, masked_value)
    peak = jnp.max(scores, axis=1)
    weights = jnp.where(visible, jnp.exp(scores - peak[:, None]), 0.0)
    totals = jnp.sum(weights, axis=1)
    summed = jnp.dot(
        weights.astype(jnp.bfloat16), keys[:, :LATENT], preferred_element_type=jnp.float32
    )
    return (summed / totals[:, None]).astype(jnp.bfloat16)


def upward(latent_out, value_up, token_count, head_count):
    head_out = jnp.einsum(
        "thl,lhd->thd",
        latent_out.reshape(token_count, head_count, LATENT),
        value_up.reshape(LATENT, head_count, VDIM),
        preferred_element_type=jnp.float32,
    )
    return head_out.astype(jnp.bfloat16).reshape(token_count, head_count * VDIM)


def body(queries_nope, queries_rope, latents, rope_keys, positions, key_up, value_up, out_proj):
    token_count = latents.shape[0]
    head_count = key_up.shape[1] // NOPE
    ctx_count = lax.axis_size("ctx")
    cosine, sine = rope_tables(positions, ROPE)
    rot_queries = rotate(
        queries_rope.astype(jnp.float32).reshape(token_count, head_count, ROPE), cosine, sine
    ).astype(jnp.bfloat16)
    rot_keys = rotate(rope_keys.astype(jnp.float32)[:, None, :], cosine, sine)[:, 0, :].astype(
        jnp.bfloat16
    )
    lat_queries = jnp.einsum(
        "thn,lhn->thl",
        queries_nope.reshape(token_count, head_count, NOPE),
        key_up.reshape(LATENT, head_count, NOPE),
        preferred_element_type=jnp.float32,
    ).astype(jnp.bfloat16)
    query_rows = jnp.concatenate([lat_queries, rot_queries], axis=-1).reshape(
        token_count * head_count, LATENT + ROPE
    )
    local_keys = jnp.concatenate([latents, rot_keys], axis=-1)
    keys = lax.all_gather(local_keys, "ctx", axis=0, tiled=True)
    first_token = lax.axis_index("ctx") * token_count
    query_index = jnp.repeat(first_token + jnp.arange(token_count, dtype=jnp.int32), head_count)
    latent_out = attend(query_rows, query_index, keys, token_count * ctx_count)
    head_out = upward(latent_out, value_up, token_count, head_count)
    partial_sums = jnp.dot(
        head_out,
        lax.all_gather(out_proj, "ctx", axis=1, tiled=True),
        preferred_element_type=jnp.float32,
    )
    return lax.psum_scatter(
        partial_sums.astype(jnp.bfloat16), "head", scatter_dimension=1, tiled=True
    )


def solution(mesh):
    in_specs = (
        P("ctx", "head"),
        P("ctx", "head"),
        P("ctx", None),
        P("ctx", None),
        P("ctx"),
        P(None, "head"),
        P(None, "head"),
        P("head", "ctx"),
    )
    out_specs = P("ctx", "head")
    return jax.shard_map(body, mesh=mesh, in_specs=in_specs, out_specs=out_specs, check_vma=False)
```

profile of v0, /device:TPU:2, one launch (start us, length us, event | category | flops | bytes accessed | tf_op | source)
XLA Modules:
  0.0 365.4 jit_solution(11109612518860116079)
XLA Ops:
  6.5 0.0 copy-start
  6.5 0.0 all-gather.3.cloned.1.call-start
  6.5 0.7 convert_element_type.33
  7.3 0.8 copy.34
  8.1 0.1 fusion.38
  8.3 0.1 copy.35
  8.4 1.5 pad_maximum_fusion.1
  9.9 0.0 all-gather.3.cloned.1.call-update
  9.9 0.0 all-gather.5.cloned.1.call-start
  9.9 0.7 all-gather.5.cloned.1.call-update
  10.6 0.0 reduce-scatter.4.cloned.1.call-start
  10.7 1.0 reshape.133
  11.7 0.1 broadcast_in_dim.24
  11.7 0.1 le.16
  11.8 0.2 multiply_cosine_fusion
  12.0 0.1 fusion.44
  12.2 0.1 subtract_convert_fusion
  12.3 0.0 copy-done
  12.3 1.4 fusion.10
  13.7 0.1 pad_maximum_fusion
  13.8 126.6 %all-gather.3.cloned.1.call-done = bf16[4096,576]{1,0:T(8,128)(2,1)} async-done(((bf16[64,576]{1,0:T(8,128)(2,1)}), bf16[4096,576]{1,0:T(8,128)(2,1)}) %all-gather.3.cloned.1.call-update) | async-done | bytes 4718608 | tf_op jit(solution)/shard_map/all_gather | solution.py:82
  140.4 6.2 %fusion = (f32[512]{0:T(512)S(1)}, f32[512,4096]{1,0:T(8,128)S(1)}) fusion(s32[512]{0:T(512)S(1)} %le.16, bf16[4096,576]{1,0:T(8,128)(2,1)} %all-gather.3.cloned.1.call-done, bf16[64,8,576]{2,0,1:T(8,128)(2,1)S(1)} %pad_maximum_fusion), kind=kOutput, calls=%fused_computation.3 | convolution fusion | flops 2424307200 | bytes 13701120 | tf_op jit(solution)/shard_map/rl,kl->rk/dot_general | solution.py:38
  146.6 0.0 copy-start.1
  146.7 2.8 fusion.1
  149.5 0.0 copy-done.1
  149.5 0.0 copy-start.2
  149.5 2.7 fusion.20
  152.3 0.0 copy-done.2
  152.3 0.5 fusion.11
  152.7 114.3 %all-gather.5.cloned.1.call-done = bf16[1024,3584]{0,1:T(8,128)(2,1)} async-done(((bf16[1024,56]{0,1:T(8,128)(2,1)}), bf16[1024,3584]{0,1:T(8,128)(2,1)}) %all-gather.5.cloned.1.call-update) | async-done | bytes 7340048 | tf_op jit(solution)/shard_map/all_gather | solution.py:89
  267.0 5.4 %convolution_convert_fusion = bf16[64,3584]{1,0:T(8,128)(2,1)S(1)} fusion(bf16[1024,3584]{0,1:T(8,128)(2,1)} %all-gather.5.cloned.1.call-done, bf16[8,8,8,128]{3,2,1,0:T(8,128)(2,1)S(1)} %fusion.11), kind=kOutput, calls=%fused_computation.6 | convolution fusion | flops 469991424 | bytes 7929856 | tf_op jit(solution)/shard_map/dot_general | solution.py:87
  272.4 1.3 copy.39
  273.7 0.0 reduce-scatter.4.cloned.1.call-update
  273.7 83.6 %reduce-scatter.4.cloned.1.call-done = bf16[448,64]{1,0:T(8,128)(2,1)} async-done(((bf16[3584,64]{1,0:T(8,128)(2,1)}), bf16[448,64]{1,0:T(8,128)(2,1)}) %reduce-scatter.4.cloned.1.call-update) | async-done | bytes 57360
  357.3 1.6 copy.40
  (4 shorter events, 0.0 us)
Async XLA Ops:
  6.5 5.8 %copy-start = (bf16[512,1024]{1,0:T(8,128)(2,1)S(1)}, bf16[512,1024]{1,0:T(8,128)(2,1)}, u32[]{:S(2)}) copy-start(bf16[512,1024]{1,0:T(8,128)(2,1)} %param.13) | copy-start | bytes 3145732
  6.5 133.9 %all-gather.3.cloned.1.call-start = ((), (), s32[]{:S(2)}) async-start(), calls=%async_computation.1 | async-start | bytes 5324800 | tf_op jit(solution)/shard_map/all_gather | solution.py:82
  9.9 257.1 %all-gather.5.cloned.1.call-start = ((), (), s32[]{:S(2)}) async-start(), calls=%async_computation.2 | async-start | bytes 7454720 | tf_op jit(solution)/shard_map/all_gather | solution.py:89
  10.6 346.6 %reduce-scatter.4.cloned.1.call-start = ((), (), s32[]{:S(2)}) async-start(), calls=%async_computation.3 | async-start | bytes 1032192
  146.6 2.9 copy-start.1
  149.5 2.8 copy-start.2
Sparse Core Ops, SparseCore 0:
  10.0 130.3 all-gather.2
  142.6 124.3 all-gather.4
  273.8 83.3 reduce-scatter.3
where the time goes:
time: 366 us; the launch traced here: 365 us
  waiting for transfers between devices  325 us (89%)
  matrix products  16.2 us (4%)
  between operations  13.2 us (4%)
  other arithmetic  5.66 us (2%)
  local copies, waits for them, and re-layouts  5.03 us (1%)
    all_gather x1, waiting for transfers between devices, body(): keys = lax.all_gather(local_keys, 'ctx', axis=0, tiled=True)  127 us
    all_gather x1, waiting for transfers between devices, body(): lax.all_gather(out_proj, 'ctx', axis=1, tiled=True)  114 us
    unnamed x4, waiting for transfers between devices  84.3 us
  transfers between devices with their start and end apart: 3, of which 3 were waited for; matrix products, arithmetic and copies ran while one was open for 4% of the time, Pallas kernels for 0%

commit v1 on v0

--- a/solution.py
+++ b/solution.py
@@ -79,7 +79,15 @@
         token_count * head_count, LATENT + ROPE
     )
     local_keys = jnp.concatenate([latents, rot_keys], axis=-1)
-    keys = lax.all_gather(local_keys, "ctx", axis=0, tiled=True)
+    keys = jnp.concatenate(
+        lax.all_to_all(
+            jnp.stack(lax.psum(1, axis_name="ctx") * [local_keys]),
+            axis_name="ctx",
+            split_axis=0,
+            concat_axis=0,
+        ),
+        axis=0,
+    )
     first_token = lax.axis_index("ctx") * token_count
     query_index = jnp.repeat(first_token + jnp.arange(token_count, dtype=jnp.int32), head_count)
     latent_out = attend(query_rows, query_index, keys, token_count * ctx_count)

time: 366 us -> 414 us (1.13)
  waiting for transfers between devices: 325 us -> 353 us
  starting transfers between devices: 0.08 us -> 17.4 us
    all_to_all x0 -> x1, waiting for transfers between devices: none -> 262 us  [body(): lax.all_to_all(jnp.stack(lax.psum(1, axis_name='ctx') * [local_keys]), ax...]
    all_gather x1 -> x0, waiting for transfers between devices: 127 us -> none  [body(): keys = lax.all_gather(local_keys, 'ctx', axis=0, tiled=True)]
    all_gather x1, waiting for transfers between devices: 114 us -> 6.75 us  [body(): lax.all_gather(out_proj, 'ctx', axis=1, tiled=True)]
    all_to_all x0 -> x1, starting transfers between devices: none -> 17.3 us  [body(): lax.all_to_all(jnp.stack(lax.psum(1, axis_name='ctx') * [local_keys]), ax...]
    unnamed x4 -> x3, waiting for transfers between devices: 84.3 us -> 84.4 us
where the time goes in v1:
time: 414 us
  waiting for transfers between devices  353 us (85%)
  matrix products  17.6 us (4%)
  starting transfers between devices  17.4 us (4%)
  between operations  13.6 us (3%)
  local copies, waits for them, and re-layouts  7.2 us (2%)
  other arithmetic  5.06 us (1%)
    all_to_all x1, waiting for transfers between devices, body(): lax.all_to_all(jnp.stack(lax.psum(1, axis_name='ctx') * [local_keys]), ax...  262 us
    unnamed x3, waiting for transfers between devices  84.4 us
    all_to_all x1, starting transfers between devices, body(): lax.all_to_all(jnp.stack(lax.psum(1, axis_name='ctx') * [local_keys]), ax...  17.3 us
  transfers between devices with their start and end apart: 3, of which 3 were waited for; matrix products, arithmetic and copies ran while one was open for 4% of the time, Pallas kernels for 0%

profile of v1, /device:TPU:2, one launch (start us, length us, event | category | flops | bytes accessed | tf_op | source)
XLA Modules:
  0.0 413.7 jit_solution(12847619730579834829)
XLA Ops:
  6.5 0.0 copy-start
  6.5 0.0 copy-start.1
  6.5 0.8 convert_element_type.33
  7.3 0.8 copy.34
  8.1 0.1 fusion.38
  8.3 0.1 copy.35
  8.4 0.9 pad_maximum_fusion.1
  9.3 0.0 copy-start.3
  9.3 3.0 stack.2
  12.3 17.3 %all-to-all-start = ((bf16[64,64,576]{2,1,0:T(8,128)(2,1)}), bf16[64,64,576]{2,1,0:T(8,128)(2,1)}, u32[]{:S(2)}, u32[]{:S(2)}) async-start(bf16[64,64,576]{2,1,0:T(8,128)(2,1)} %stack.2), calls=%async_computation | async-start | bytes 10485760 | tf_op jit(solution)/shard_map/all_to_all | solution.py:83
  29.6 0.0 all-gather.2.cloned.1.call-start
  29.7 0.7 all-gather.2.cloned.1.call-update
  30.4 0.0 reduce-scatter.4.cloned.1.call-start
  30.4 0.0 copy-done.1
  30.4 0.1 reshape.139
  30.6 0.1 broadcast_in_dim.24
  30.6 0.1 le.16
  30.7 0.2 multiply_cosine_fusion
  30.9 0.1 fusion.44
  31.1 0.1 subtract_convert_fusion
  31.2 0.0 copy-done
  31.2 0.0 copy-done.3
  31.2 0.5 fusion.10
  31.7 0.1 pad_maximum_fusion
  31.8 261.8 %all-to-all-done = bf16[64,64,576]{2,1,0:T(8,128)(2,1)} async-done(((bf16[64,64,576]{2,1,0:T(8,128)(2,1)}), bf16[64,64,576]{2,1,0:T(8,128)(2,1)}, u32[]{:S(2)}, u32[]{:S(2)}) %all-to-all-start) | async-done | bytes 4718624 | tf_op jit(solution)/shard_map/all_to_all | solution.py:83
  293.6 6.2 %fusion = (f32[512]{0:T(512)S(1)}, f32[512,4096]{1,0:T(8,128)S(1)}) fusion(s32[512]{0:T(512)S(1)} %le.16, bf16[4096,576]{1,0:T(8,128)(2,1)} %bitcast.5, bf16[64,8,576]{2,0,1:T(8,128)(2,1)S(1)} %pad_maximum_fusion), kind=kOutput, calls=%fused_computation.3 | convolution fusion | flops 2424307200 | bytes 13701120 | tf_op jit(solution)/shard_map/rl,kl->rk/dot_general | solution.py:38
  299.8 2.8 fusion.1
  302.6 0.0 copy-start.2
  302.6 5.0 %fusion.20 = bf16[64,8,512]{2,1,0:T(8,128)(2,1)S(1)} fusion(bf16[4096,576]{1,0:T(8,128)(2,1)} %bitcast.5, f32[512,4096]{1,0:T(8,128)S(1)} %get-tuple-element.14, f32[512]{0:T(512)S(1)} %get-tuple-element.13, s32[512]{0:T(512)S(1)} %le.16, f32[512]{0:T(512)S(1)} %fusion.1), kind=kOutput, calls=%fused_computation.22 | convolution fusion | flops 2160590848 | bytes 13113344 | tf_op jit(solution)/shard_map/dot_general | solution.py:45
  307.7 0.0 copy-done.2
  307.7 0.5 fusion.11
  308.1 6.8 %all-gather.2.cloned.1.call-done = bf16[1024,3584]{0,1:T(8,128)(2,1)} async-done(((bf16[1024,56]{0,1:T(8,128)(2,1)}), bf16[1024,3584]{0,1:T(8,128)(2,1)}) %all-gather.2.cloned.1.call-update) | async-done | bytes 7340048 | tf_op jit(solution)/shard_map/all_gather | solution.py:97
  314.9 5.4 %convolution_convert_fusion = bf16[64,3584]{1,0:T(8,128)(2,1)S(1)} fusion(bf16[1024,3584]{0,1:T(8,128)(2,1)} %all-gather.2.cloned.1.call-done, bf16[8,8,8,128]{3,2,1,0:T(8,128)(2,1)S(1)} %fusion.11), kind=kOutput, calls=%fused_computation.6 | convolution fusion | flops 469991424 | bytes 7929856 | tf_op jit(solution)/shard_map/dot_general | solution.py:95
  320.3 1.3 copy.39
  321.6 0.0 reduce-scatter.4.cloned.1.call-update
  321.6 83.7 %reduce-scatter.4.cloned.1.call-done = bf16[448,64]{1,0:T(8,128)(2,1)} async-done(((bf16[3584,64]{1,0:T(8,128)(2,1)}), bf16[448,64]{1,0:T(8,128)(2,1)}) %reduce-scatter.4.cloned.1.call-update) | async-done | bytes 57360
  405.3 1.6 copy.40
  (4 shorter events, 0.0 us)
Async XLA Ops:
  6.5 24.6 %copy-start = (bf16[512,1024]{1,0:T(8,128)(2,1)S(1)}, bf16[512,1024]{1,0:T(8,128)(2,1)}, u32[]{:S(2)}) copy-start(bf16[512,1024]{1,0:T(8,128)(2,1)} %param.13) | copy-start | bytes 3145732
  6.5 23.9 %copy-start.1 = (bf16[64,512]{1,0:T(8,128)(2,1)S(1)}, bf16[64,512]{1,0:T(8,128)(2,1)}, u32[]{:S(2)}) copy-start(bf16[64,512]{1,0:T(8,128)(2,1)} %param.9) | copy-start | bytes 196612
  9.3 21.9 %copy-start.3 = (bf16[64,1024]{1,0:T(8,128)(2,1)S(1)}, bf16[64,1024]{1,0:T(8,128)(2,1)}, u32[]{:S(2)}) copy-start(bf16[64,1024]{1,0:T(8,128)(2,1)} %param.8) | copy-start | bytes 393220
  12.3 281.3 %all-to-all-start = ((bf16[64,64,576]{2,1,0:T(8,128)(2,1)}), bf16[64,64,576]{2,1,0:T(8,128)(2,1)}, u32[]{:S(2)}, u32[]{:S(2)}) async-start(bf16[64,64,576]{2,1,0:T(8,128)(2,1)} %stack.2), calls=%async_computation | async-start | bytes 10485760 | tf_op jit(solution)/shard_map/all_to_all | solution.py:83
  29.6 285.3 %all-gather.2.cloned.1.call-start = ((), (), s32[]{:S(2)}) async-start(), calls=%async_computation.2 | async-start | bytes 7454720 | tf_op jit(solution)/shard_map/all_gather | solution.py:97
  30.4 374.9 %reduce-scatter.4.cloned.1.call-start = ((), (), s32[]{:S(2)}) async-start(), calls=%async_computation.3 | async-start | bytes 1032192
  302.6 5.1 %copy-start.2 = (bf16[512,1024]{1,0:T(8,128)(2,1)S(1)}, bf16[512,1024]{1,0:T(8,128)(2,1)}, u32[]{:S(2)}) copy-start(bf16[512,1024]{1,0:T(8,128)(2,1)} %param.14) | copy-start | bytes 3145732
Sparse Core Ops, SparseCore 0:
  32.6 282.2 all-gather.1
  321.7 83.5 reduce-scatter.3
